TPU v7x, 256 devices: a whole 4x4x8 slice. The times are simulated.
256 devices in a mesh: seq: 32 (over x, z), tp: 8 (over y, core).
Axes of the slice: x: 4, y: 4, z: 8, core: 2. Of those that a mesh axis runs over, the one named last changes fastest.
Arguments:
- tokens: bfloat16 [32768, 2048], P('seq', 'tp'), may hold values from -6 to 6
- w_inner: bfloat16 [2048, 2, 4096], P('seq', None, 'tp'), may hold values from -0.125 to 0.125
- w_states: bfloat16 [2048, 256], P('seq'), may hold values from -0.125 to 0.125
- w_step: bfloat16 [2048, 64], P('seq', 'tp'), may hold values from -0.125 to 0.125
- conv_inner: float32 [4, 4096], P(None, 'tp'), may hold values from -3 to 3
- conv_states: float32 [4, 256], replicated, may hold values from -3 to 3
- decay_rate: float32 [64], P('tp'), may hold values from 0 to 1, as said below
- step_bias: float32 [64], P('tp'), may hold values from -1 to 0.5
- skip_gain: float32 [64], P('tp'), may hold values from 0.5 to 1.5
- norm_gain: float32 [4096], P('tp'), may hold values from 0.5 to 1.5
- w_output: bfloat16 [4096, 2048], P('tp', 'seq'), may hold values from -0.09375 to 0.09375
- block_owner: int32 [128], replicated, may hold values from 0 to 19, as said below
- lengths: int32 [20], replicated, may hold values from 1 to 16384, as said below
Outputs:
- mixed: bfloat16 [32768, 2048], P('seq', 'tp')
Inputs may be any that keep to these rules, and one draw needn't show every extreme that they name: `block_owner`: each prompt's blocks are consecutive, prompt r has ceil(lengths[r] / 256) of them, and the prompts follow one another in an order drawn afresh; one prompt has 64 blocks and is neither the first nor the last in that order. `lengths`: one prompt has exactly 16384 tokens. `decay_rate`: Positive.
All inputs are finite; a program needn't handle non-finite values.
Results may differ from a plain program's by a relative error of at most 0.0075.
Values may be sent and summed in bfloat16 or wider, within the bound.
No kernel may reach another device: no remote copies, remote signals or barrier semaphores. Data moves between devices by JAX's collectives and lax.ppermute only.
A program may use at most 64 MiB of HBM per device.

v0:
```python
import jax
import jax.numpy as jnp
from jax import lax
from jax.sharding import PartitionSpec as P

BLOCK = 256


def passed_along(value, axis, by):
    count = lax.axis_size(axis)
    pairs = [(i, i + by) for i in range(count) if 0 <= i + by < count]
    return lax.ppermute(value, axis, pairs)


def convolve(values, edge_rows, weights, in_block, carry_on):
    lag_rows = weights.shape[0] - 1
    row_total = values.shape[0]
    widened = jnp.concatenate([edge_rows, values], axis=0).astype(jnp.float32)
    total = jnp.zeros(values.shape, jnp.float32)
    for offset in range(weights.shape[0]):
        shifted = widened[lag_rows - offset : lag_rows - offset + row_total]
        keeping = (in_block >= offset) | carry_on
        total = total + jnp.where(keeping[:, None], shifted, 0.0) * weights[offset]
    return jax.nn.silu(total).astype(jnp.bfloat16)


def on_device(
    tokens,
    w_inner,
    w_states,
    w_step,
    conv_inner,
    conv_states,
    decay_rate,
    step_bias,
    skip_gain,
    norm_gain,
    w_output,
    block_owner,
    lengths,
):
    row_count = tokens.shape[0]
    local_blocks = row_count // BLOCK
    total_blocks = block_owner.shape[0]
    heads_here = w_step.shape[1]
    inner_here = w_inner.shape[2]
    state_size = w_states.shape[1] // 2
    head_size = inner_here // heads_here
    lag_rows = conv_inner.shape[0] - 1
    block_ids = jnp.arange(total_blocks, dtype=jnp.int32)
    same_owner = block_owner[:, None] == block_owner[None, :]
    first_block = jnp.min(jnp.where(same_owner, block_ids[None, :], total_blocks), axis=1)
    starting = (first_block == block_ids).astype(jnp.int32)
    request_ids = jnp.arange(lengths.shape[0], dtype=jnp.int32)
    own_length = jnp.sum(
        jnp.where(block_owner[:, None] == request_ids[None, :], lengths[None, :], 0), axis=1
    )
    valid_rows = jnp.clip(own_length - (block_ids - first_block) * BLOCK, 0, BLOCK)
    seq_index = lax.axis_index("seq")
    local_start = lax.dynamic_slice_in_dim(starting, seq_index * local_blocks, local_blocks)
    local_valid = lax.dynamic_slice_in_dim(valid_rows, seq_index * local_blocks, local_blocks)
    in_block = jnp.arange(row_count, dtype=jnp.int32) % BLOCK
    carry_on = jnp.repeat(local_start == 0, BLOCK)
    whole = lax.all_gather(tokens, "tp", axis=1, tiled=True)
    pieces = (
        lax.all_gather(w_inner, "seq", axis=0, tiled=True),
        lax.all_gather(w_states, "seq", axis=0, tiled=True),
        lax.all_gather(w_step, "seq", axis=0, tiled=True),
    )
    count = pieces[0].shape[0]
    inner_sum = jnp.dot(
        whole, pieces[0].reshape(count, 2 * inner_here), preferred_element_type=jnp.float32
    )
    states_sum = jnp.dot(whole, pieces[1], preferred_element_type=jnp.float32)
    step_sum = jnp.dot(whole, pieces[2], preferred_element_type=jnp.float32)
    projected = inner_sum.astype(jnp.bfloat16)
    gate_in = projected[:, :inner_here]
    x_in = projected[:, inner_here:]
    bc_in = states_sum.astype(jnp.bfloat16)
    step_raw = step_sum.astype(jnp.bfloat16)
    edge_inner, edge_states = passed_along(
        (x_in[row_count - lag_rows :], bc_in[row_count - lag_rows :]), "seq", 1
    )
    x_conv = convolve(x_in, edge_inner, conv_inner, in_block, carry_on)
    bc_conv = convolve(bc_in, edge_states, conv_states, in_block, carry_on)
    step_size = jax.nn.softplus(step_raw.astype(jnp.float32) + step_bias)
    log_decay = -decay_rate * step_size
    x_heads = x_conv.reshape(local_blocks, BLOCK, heads_here, head_size)
    b_rows = bc_conv[:, :state_size].reshape(local_blocks, BLOCK, state_size)
    c_rows = bc_conv[:, state_size:].reshape(local_blocks, BLOCK, state_size)
    step_blocks = step_size.reshape(local_blocks, BLOCK, heads_here)
    cumulative = jnp.cumsum(log_decay.reshape(local_blocks, BLOCK, heads_here), axis=1)
    causal = jnp.arange(BLOCK)[:, None] >= jnp.arange(BLOCK)[None, :]
    spread = cumulative[:, :, None, :] - cumulative[:, None, :, :]
    decays = jnp.exp(jnp.where(causal[None, :, :, None], spread, -jnp.inf))
    intersection = jnp.einsum("cin,cjn->cij", c_rows, b_rows, preferred_element_type=jnp.float32)
    mixing = (decays * intersection[:, :, :, None] * step_blocks[:, None, :, :]).astype(
        jnp.bfloat16
    )
    y_inner = jnp.einsum("cijh,cjhp->cihp", mixing, x_heads, preferred_element_type=jnp.float32)
    final_log = cumulative[:, -1, :]
    tail_weight = jnp.exp(final_log[:, None, :] - cumulative) * step_blocks
    weighted_b = (tail_weight[:, :, :, None] * b_rows.astype(jnp.float32)[:, :, None, :]).astype(
        jnp.bfloat16
    )
    fresh = jnp.einsum("cjhn,cjhp->chnp", weighted_b, x_heads, preferred_element_type=jnp.float32)
    keep_flag = jnp.where(local_start == 1, 0.0, 1.0).astype(jnp.float32)
    block_gain_each = jnp.exp(final_log) * keep_flag[:, None]

    def fold_block(carry, item):
        gain_now, fresh_now = item
        return ((carry[0] * gain_now, gain_now[:, None, None] * carry[1] + fresh_now), None)

    zero_state = jnp.zeros((heads_here, state_size, head_size), jnp.float32)
    unit_gain = jnp.ones((heads_here,), jnp.float32)
    (block_gain, block_state), _ = lax.scan(
        fold_block, (unit_gain, zero_state), (block_gain_each, fresh)
    )

    def relay(iteration, entering_now):
        return passed_along(block_gain[:, None, None] * entering_now + block_state, "seq", 1)

    entering = lax.fori_loop(0, lax.axis_size("seq") - 1, relay, zero_state)

    def pass_block(previous, item):
        log_now, keep_now, fresh_now = item
        incoming = previous * keep_now
        return (jnp.exp(log_now)[:, None, None] * incoming + fresh_now, incoming)

    _, incoming_all = lax.scan(pass_block, entering, (final_log, keep_flag, fresh))
    incoming_half = incoming_all.astype(jnp.bfloat16)
    y_carry = jnp.exp(cumulative)[:, :, :, None] * jnp.einsum(
        "cin,chnp->cihp", c_rows, incoming_half, preferred_element_type=jnp.float32
    )
    y_total = (y_inner + y_carry).reshape(row_count, inner_here) + jnp.repeat(skip_gain, head_size)[
        None, :
    ] * x_conv.astype(jnp.float32)
    gated = y_total * jax.nn.silu(gate_in.astype(jnp.float32))
    squares = lax.psum(jnp.sum(gated * gated, axis=1), "tp")
    square_mean = squares / (inner_here * lax.axis_size("tp"))
    normed = (gated * lax.rsqrt(square_mean + 1e-05)[:, None] * norm_gain).astype(jnp.bfloat16)
    partial_out = jnp.dot(
        normed,
        lax.all_gather(w_output, "seq", axis=1, tiled=True),
        preferred_element_type=jnp.float32,
    )
    summed = lax.psum_scatter(partial_out, "tp", scatter_dimension=1, tiled=True)
    live = in_block < jnp.repeat(local_valid, BLOCK)
    return jnp.where(live[:, None], summed, 0.0).astype(jnp.bfloat16)


def solution(mesh):
    return jax.shard_map(
        on_device,
        mesh=mesh,
        in_specs=(
            P("seq", "tp"),
            P("seq", None, "tp"),
            P("seq", None),
            P("seq", "tp"),
            P(None, "tp"),
            P(),
            P("tp"),
            P("tp"),
            P("tp"),
            P("tp"),
            P("tp", "seq"),
            P(),
            P(),
        ),
        out_specs=P("seq", "tp"),
        check_vma=False,
    )
```

profile of v0, /device:TPU:1, one launch (start us, length us, event | category | flops | bytes accessed | tf_op | source)
XLA Modules:
  0.0 875.8 jit_solution(9368195072958447139)
XLA Ops:
  13.4 41.9 %all-gather = bf16[32,64,8]{1,2,0:T(8,128)(2,1)S(1)} all-gather(bf16[1,64,8]{1,2,0:T(8,128)(2,1)} %bitcast.99), channel_id=1, replica_groups=mesh['seq'=32,'tp'=8] {'seq'}, dimensions={0}, use_global_device_ids=true | all-gather | bytes 33792 | tf_op jit(solution)/shard_map/all_gather | solution.py:68
  57.5 27.5 %all-gather.10.cloned.1.call-done = bf16[2048,256]{1,0:T(8,128)(2,1)} async-done(((bf16[64,256]{1,0:T(8,128)(2,1)}), bf16[2048,256]{1,0:T(8,128)(2,1)}) %all-gather.10.cloned.1.call-update) | async-done | bytes 1048592 | tf_op jit(solution)/shard_map/all_gather | solution.py:67
  85.0 42.9 %all-gather.6.cloned.1.call-done = bf16[1024,2048]{1,0:T(8,128)(2,1)} async-done(((bf16[1024,256]{1,0:T(8,128)(2,1)}), bf16[1024,2048]{1,0:T(8,128)(2,1)}) %all-gather.6.cloned.1.call-update) | async-done | bytes 4194320 | tf_op jit(solution)/shard_map/all_gather | solution.py:64
  141.9 67.3 %all-gather.8.cloned.1.call-done = bf16[2048,2,512]{2,1,0:T(2,128)(2,1)} async-done(((bf16[64,2,512]{2,1,0:T(2,128)(2,1)}), bf16[2048,2,512]{2,1,0:T(2,128)(2,1)}) %all-gather.8.cloned.1.call-update) | async-done | bytes 4194320 | tf_op jit(solution)/shard_map/all_gather | solution.py:66
  245.5 454.9 %while.35 = (s32[]{:T(128)}, f32[8,128,64]{2,1,0:T(8,128)S(1)}, f32[8]{0:T(128)S(1)}, f32[8,128,64]{2,1,0:T(8,128)S(1)}, s32[]{:T(128)}) while((s32[]{:T(128)}, f32[8,128,64]{2,1,0:T(8,128)S(1)}, f32[8]{0:T(128)S(1)}, f32[8,128,64]{2,1,0:T(8,128)S(1)}, s32[]{:T(128)}) %tuple.77), condition=%wide.region_7.8_spmd, body=%wide.region_6.7_spmd.sunk | while | flops 131074 | bytes 1835141 | solution.py:123
  249.8 7.4 collective-permute-done
  262.2 9.9 %collective-permute-done = f32[8,128,64]{2,1,0:T(8,128)S(1)} collective-permute-done((f32[8,128,64]{2,1,0:T(8,128)}, f32[8,128,64]{2,1,0:T(8,128)S(1)}, u32[]{:S(2)}, u32[]{:S(2)}) %collective-permute-start) | collective-permute-done | bytes 262176 | tf_op jit(solution)/shard_map/while/body/eval_jaxpr/ppermute | solution.py:12
  277.4 11.2 %collective-permute-done = f32[8,128,64]{2,1,0:T(8,128)S(1)} collective-permute-done((f32[8,128,64]{2,1,0:T(8,128)}, f32[8,128,64]{2,1,0:T(8,128)S(1)}, u32[]{:S(2)}, u32[]{:S(2)}) %collective-permute-start) | collective-permute-done | bytes 262176 | tf_op jit(solution)/shard_map/while/body/eval_jaxpr/ppermute | solution.py:12
  316.6 8.4 collective-permute-done
  329.6 9.5 %collective-permute-done = f32[8,128,64]{2,1,0:T(8,128)S(1)} collective-permute-done((f32[8,128,64]{2,1,0:T(8,128)}, f32[8,128,64]{2,1,0:T(8,128)S(1)}, u32[]{:S(2)}, u32[]{:S(2)}) %collective-permute-start) | collective-permute-done | bytes 262176 | tf_op jit(solution)/shard_map/while/body/eval_jaxpr/ppermute | solution.py:12
  343.8 10.7 %collective-permute-done = f32[8,128,64]{2,1,0:T(8,128)S(1)} collective-permute-done((f32[8,128,64]{2,1,0:T(8,128)}, f32[8,128,64]{2,1,0:T(8,128)S(1)}, u32[]{:S(2)}, u32[]{:S(2)}) %collective-permute-start) | collective-permute-done | bytes 262176 | tf_op jit(solution)/shard_map/while/body/eval_jaxpr/ppermute | solution.py:12
  359.2 11.8 %collective-permute-done = f32[8,128,64]{2,1,0:T(8,128)S(1)} collective-permute-done((f32[8,128,64]{2,1,0:T(8,128)}, f32[8,128,64]{2,1,0:T(8,128)S(1)}, u32[]{:S(2)}, u32[]{:S(2)}) %collective-permute-start) | collective-permute-done | bytes 262176 | tf_op jit(solution)/shard_map/while/body/eval_jaxpr/ppermute | solution.py:12
  376.7 12.0 %collective-permute-done = f32[8,128,64]{2,1,0:T(8,128)S(1)} collective-permute-done((f32[8,128,64]{2,1,0:T(8,128)}, f32[8,128,64]{2,1,0:T(8,128)S(1)}, u32[]{:S(2)}, u32[]{:S(2)}) %collective-permute-start) | collective-permute-done | bytes 262176 | tf_op jit(solution)/shard_map/while/body/eval_jaxpr/ppermute | solution.py:12
  394.9 10.9 %collective-permute-done = f32[8,128,64]{2,1,0:T(8,128)S(1)} collective-permute-done((f32[8,128,64]{2,1,0:T(8,128)}, f32[8,128,64]{2,1,0:T(8,128)S(1)}, u32[]{:S(2)}, u32[]{:S(2)}) %collective-permute-start) | collective-permute-done | bytes 262176 | tf_op jit(solution)/shard_map/while/body/eval_jaxpr/ppermute | solution.py:12
  411.4 9.8 %collective-permute-done = f32[8,128,64]{2,1,0:T(8,128)S(1)} collective-permute-done((f32[8,128,64]{2,1,0:T(8,128)}, f32[8,128,64]{2,1,0:T(8,128)S(1)}, u32[]{:S(2)}, u32[]{:S(2)}) %collective-permute-start) | collective-permute-done | bytes 262176 | tf_op jit(solution)/shard_map/while/body/eval_jaxpr/ppermute | solution.py:12
  426.1 8.6 collective-permute-done
  440.9 7.8 collective-permute-done
  519.0 8.3 collective-permute-done
  533.0 8.7 collective-permute-done
  548.7 9.5 %collective-permute-done = f32[8,128,64]{2,1,0:T(8,128)S(1)} collective-permute-done((f32[8,128,64]{2,1,0:T(8,128)}, f32[8,128,64]{2,1,0:T(8,128)S(1)}, u32[]{:S(2)}, u32[]{:S(2)}) %collective-permute-start) | collective-permute-done | bytes 262176 | tf_op jit(solution)/shard_map/while/body/eval_jaxpr/ppermute | solution.py:12
  566.1 10.6 %collective-permute-done = f32[8,128,64]{2,1,0:T(8,128)S(1)} collective-permute-done((f32[8,128,64]{2,1,0:T(8,128)}, f32[8,128,64]{2,1,0:T(8,128)S(1)}, u32[]{:S(2)}, u32[]{:S(2)}) %collective-permute-start) | collective-permute-done | bytes 262176 | tf_op jit(solution)/shard_map/while/body/eval_jaxpr/ppermute | solution.py:12
  577.7 7.6 collective-permute-start
  585.3 11.8 %collective-permute-done = f32[8,128,64]{2,1,0:T(8,128)S(1)} collective-permute-done((f32[8,128,64]{2,1,0:T(8,128)}, f32[8,128,64]{2,1,0:T(8,128)S(1)}, u32[]{:S(2)}, u32[]{:S(2)}) %collective-permute-start) | collective-permute-done | bytes 262176 | tf_op jit(solution)/shard_map/while/body/eval_jaxpr/ppermute | solution.py:12
  598.0 7.7 collective-permute-start
  605.7 11.1 %collective-permute-done = f32[8,128,64]{2,1,0:T(8,128)S(1)} collective-permute-done((f32[8,128,64]{2,1,0:T(8,128)}, f32[8,128,64]{2,1,0:T(8,128)S(1)}, u32[]{:S(2)}, u32[]{:S(2)}) %collective-permute-start) | collective-permute-done | bytes 262176 | tf_op jit(solution)/shard_map/while/body/eval_jaxpr/ppermute | solution.py:12
  624.5 9.9 %collective-permute-done = f32[8,128,64]{2,1,0:T(8,128)S(1)} collective-permute-done((f32[8,128,64]{2,1,0:T(8,128)}, f32[8,128,64]{2,1,0:T(8,128)S(1)}, u32[]{:S(2)}, u32[]{:S(2)}) %collective-permute-start) | collective-permute-done | bytes 262176 | tf_op jit(solution)/shard_map/while/body/eval_jaxpr/ppermute | solution.py:12
  641.4 8.8 %collective-permute-done = f32[8,128,64]{2,1,0:T(8,128)S(1)} collective-permute-done((f32[8,128,64]{2,1,0:T(8,128)}, f32[8,128,64]{2,1,0:T(8,128)S(1)}, u32[]{:S(2)}, u32[]{:S(2)}) %collective-permute-start) | collective-permute-done | bytes 262176 | tf_op jit(solution)/shard_map/while/body/eval_jaxpr/ppermute | solution.py:12
  656.4 7.6 collective-permute-done
  700.5 15.3 %while.36 = (s32[]{:T(128)}, f32[8,128,64]{2,1,0:T(8,128)S(1)}, bf16[4,8,128,64]{3,2,1,0:T(8,128)(2,1)}, f32[4,8]{1,0:T(4,128)S(1)}, f32[4]{0:T(128)S(1)}, /*index=5*/f32[4,8,128,64]{3,2,1,0:T(8,128)}, s32[]{:T(128)}) while((s32[]{:T(128)}, f32[8,128,64]{2,1,0:T(8,128)S(1)}, bf16[4,8,128,64]{3,2,1,0:T(8,128)(2,1)}, f32[4,8]{1,0:T(4,128)S(1)}, ...), condition=%wide.region_9.10_spmd, body=%wide.region_8.9_spmd.sunk | while | flops 262146 | bytes 1574085 | solution.py:130
  737.1 48.3 %psum.7 = f32[1024]{0:T(1024)S(1)} all-reduce(f32[1024]{0:T(1024)S(1)} %get-tuple-element.196), channel_id=1, replica_groups=mesh['seq'=32,'tp'=8] {'tp'}, use_global_device_ids=true, to_apply=%region_11.12 | all-reduce | flops 1024 | bytes 8192 | tf_op jit(solution)/shard_map/psum | solution.py:139
  785.4 7.9 fusion.26
  794.3 72.8 %reduce-scatter.2.cloned.1.call-done = f32[1024,256]{1,0:T(8,128)} async-done(((f32[1024,2048]{1,0:T(8,128)}), f32[1024,256]{1,0:T(8,128)}) %reduce-scatter.2.cloned.1.call-update) | async-done | bytes 1048592 | tf_op jit(solution)/shard_map/reduce_scatter | solution.py:147
  (212 shorter events, 340.8 us)
Async XLA Ops:
  6.5 78.4 %all-gather.10.cloned.1.call-start = ((), (), s32[]{:S(2)}) async-start(), calls=%async_computation.3 | async-start | bytes 1081344 | tf_op jit(solution)/shard_map/all_gather | solution.py:67
  7.3 120.7 %all-gather.6.cloned.1.call-start = ((), (), s32[]{:S(2)}) async-start(), calls=%async_computation.1 | async-start | bytes 4718592 | tf_op jit(solution)/shard_map/all_gather | solution.py:64
  8.0 201.3 %all-gather.8.cloned.1.call-start = ((), (), s32[]{:S(2)}) async-start(), calls=%async_computation.2 | async-start | bytes 4325376 | tf_op jit(solution)/shard_map/all_gather | solution.py:66
  8.7 776.7 %all-gather.12.cloned.1.call-start = ((), (), s32[]{:S(2)}) async-start(), calls=%async_computation.4 | async-start | bytes 2162688 | tf_op jit(solution)/shard_map/all_gather | solution.py:144
  9.3 857.7 %reduce-scatter.2.cloned.1.call-start = ((), (), s32[]{:S(2)}) async-start(), calls=%async_computation.5 | async-start | bytes 9437184 | tf_op jit(solution)/shard_map/reduce_scatter | solution.py:147
  258.1 14.0 %collective-permute-start = (f32[8,128,64]{2,1,0:T(8,128)}, f32[8,128,64]{2,1,0:T(8,128)S(1)}, u32[]{:S(2)}, u32[]{:S(2)}) collective-permute-start(f32[8,128,64]{2,1,0:T(8,128)} %multiply_add_fusion.2), channel_id=1, source_target_pairs={{0,8},{8,16},{16,24},{24,32},{32,40},{40,48},{48,56},{56,64},{64,7... | collective-permute-start | bytes 786440 | tf_op jit(solution)/shard_map/while/body/eval_jaxpr/ppermute | solution.py:12
  273.0 15.6 %collective-permute-start = (f32[8,128,64]{2,1,0:T(8,128)}, f32[8,128,64]{2,1,0:T(8,128)S(1)}, u32[]{:S(2)}, u32[]{:S(2)}) collective-permute-start(f32[8,128,64]{2,1,0:T(8,128)} %multiply_add_fusion.2), channel_id=1, source_target_pairs={{0,8},{8,16},{16,24},{24,32},{32,40},{40,48},{48,56},{56,64},{64,7... | collective-permute-start | bytes 786440 | tf_op jit(solution)/shard_map/while/body/eval_jaxpr/ppermute | solution.py:12
  312.9 12.1 %collective-permute-start = (f32[8,128,64]{2,1,0:T(8,128)}, f32[8,128,64]{2,1,0:T(8,128)S(1)}, u32[]{:S(2)}, u32[]{:S(2)}) collective-permute-start(f32[8,128,64]{2,1,0:T(8,128)} %multiply_add_fusion.2), channel_id=1, source_target_pairs={{0,8},{8,16},{16,24},{24,32},{32,40},{40,48},{48,56},{56,64},{64,7... | collective-permute-start | bytes 786440 | tf_op jit(solution)/shard_map/while/body/eval_jaxpr/ppermute | solution.py:12
  325.9 13.3 %collective-permute-start = (f32[8,128,64]{2,1,0:T(8,128)}, f32[8,128,64]{2,1,0:T(8,128)S(1)}, u32[]{:S(2)}, u32[]{:S(2)}) collective-permute-start(f32[8,128,64]{2,1,0:T(8,128)} %multiply_add_fusion.2), channel_id=1, source_target_pairs={{0,8},{8,16},{16,24},{24,32},{32,40},{40,48},{48,56},{56,64},{64,7... | collective-permute-start | bytes 786440 | tf_op jit(solution)/shard_map/while/body/eval_jaxpr/ppermute | solution.py:12
  340.1 14.4 %collective-permute-start = (f32[8,128,64]{2,1,0:T(8,128)}, f32[8,128,64]{2,1,0:T(8,128)S(1)}, u32[]{:S(2)}, u32[]{:S(2)}) collective-permute-start(f32[8,128,64]{2,1,0:T(8,128)} %multiply_add_fusion.2), channel_id=1, source_target_pairs={{0,8},{8,16},{16,24},{24,32},{32,40},{40,48},{48,56},{56,64},{64,7... | collective-permute-start | bytes 786440 | tf_op jit(solution)/shard_map/while/body/eval_jaxpr/ppermute | solution.py:12
  355.4 15.6 %collective-permute-start = (f32[8,128,64]{2,1,0:T(8,128)}, f32[8,128,64]{2,1,0:T(8,128)S(1)}, u32[]{:S(2)}, u32[]{:S(2)}) collective-permute-start(f32[8,128,64]{2,1,0:T(8,128)} %multiply_add_fusion.2), channel_id=1, source_target_pairs={{0,8},{8,16},{16,24},{24,32},{32,40},{40,48},{48,56},{56,64},{64,7... | collective-permute-start | bytes 786440 | tf_op jit(solution)/shard_map/while/body/eval_jaxpr/ppermute | solution.py:12
  371.9 16.8 %collective-permute-start = (f32[8,128,64]{2,1,0:T(8,128)}, f32[8,128,64]{2,1,0:T(8,128)S(1)}, u32[]{:S(2)}, u32[]{:S(2)}) collective-permute-start(f32[8,128,64]{2,1,0:T(8,128)} %multiply_add_fusion.2), channel_id=1, source_target_pairs={{0,8},{8,16},{16,24},{24,32},{32,40},{40,48},{48,56},{56,64},{64,7... | collective-permute-start | bytes 786440 | tf_op jit(solution)/shard_map/while/body/eval_jaxpr/ppermute | solution.py:12
  389.6 16.3 %collective-permute-start = (f32[8,128,64]{2,1,0:T(8,128)}, f32[8,128,64]{2,1,0:T(8,128)S(1)}, u32[]{:S(2)}, u32[]{:S(2)}) collective-permute-start(f32[8,128,64]{2,1,0:T(8,128)} %multiply_add_fusion.2), channel_id=1, source_target_pairs={{0,8},{8,16},{16,24},{24,32},{32,40},{40,48},{48,56},{56,64},{64,7... | collective-permute-start | bytes 786440 | tf_op jit(solution)/shard_map/while/body/eval_jaxpr/ppermute | solution.py:12
  406.7 14.4 %collective-permute-start = (f32[8,128,64]{2,1,0:T(8,128)}, f32[8,128,64]{2,1,0:T(8,128)S(1)}, u32[]{:S(2)}, u32[]{:S(2)}) collective-permute-start(f32[8,128,64]{2,1,0:T(8,128)} %multiply_add_fusion.2), channel_id=1, source_target_pairs={{0,8},{8,16},{16,24},{24,32},{32,40},{40,48},{48,56},{56,64},{64,7... | collective-permute-start | bytes 786440 | tf_op jit(solution)/shard_map/while/body/eval_jaxpr/ppermute | solution.py:12
  422.1 12.7 %collective-permute-start = (f32[8,128,64]{2,1,0:T(8,128)}, f32[8,128,64]{2,1,0:T(8,128)S(1)}, u32[]{:S(2)}, u32[]{:S(2)}) collective-permute-start(f32[8,128,64]{2,1,0:T(8,128)} %multiply_add_fusion.2), channel_id=1, source_target_pairs={{0,8},{8,16},{16,24},{24,32},{32,40},{40,48},{48,56},{56,64},{64,7... | collective-permute-start | bytes 786440 | tf_op jit(solution)/shard_map/while/body/eval_jaxpr/ppermute | solution.py:12
  435.7 13.0 %collective-permute-start = (f32[8,128,64]{2,1,0:T(8,128)}, f32[8,128,64]{2,1,0:T(8,128)S(1)}, u32[]{:S(2)}, u32[]{:S(2)}) collective-permute-start(f32[8,128,64]{2,1,0:T(8,128)} %multiply_add_fusion.2), channel_id=1, source_target_pairs={{0,8},{8,16},{16,24},{24,32},{32,40},{40,48},{48,56},{56,64},{64,7... | collective-permute-start | bytes 786440 | tf_op jit(solution)/shard_map/while/body/eval_jaxpr/ppermute | solution.py:12
  449.6 12.2 %collective-permute-start = (f32[8,128,64]{2,1,0:T(8,128)}, f32[8,128,64]{2,1,0:T(8,128)S(1)}, u32[]{:S(2)}, u32[]{:S(2)}) collective-permute-start(f32[8,128,64]{2,1,0:T(8,128)} %multiply_add_fusion.2), channel_id=1, source_target_pairs={{0,8},{8,16},{16,24},{24,32},{32,40},{40,48},{48,56},{56,64},{64,7... | collective-permute-start | bytes 786440 | tf_op jit(solution)/shard_map/while/body/eval_jaxpr/ppermute | solution.py:12
  462.7 11.6 %collective-permute-start = (f32[8,128,64]{2,1,0:T(8,128)}, f32[8,128,64]{2,1,0:T(8,128)S(1)}, u32[]{:S(2)}, u32[]{:S(2)}) collective-permute-start(f32[8,128,64]{2,1,0:T(8,128)} %multiply_add_fusion.2), channel_id=1, source_target_pairs={{0,8},{8,16},{16,24},{24,32},{32,40},{40,48},{48,56},{56,64},{64,7... | collective-permute-start | bytes 786440 | tf_op jit(solution)/shard_map/while/body/eval_jaxpr/ppermute | solution.py:12
  475.2 11.6 %collective-permute-start = (f32[8,128,64]{2,1,0:T(8,128)}, f32[8,128,64]{2,1,0:T(8,128)S(1)}, u32[]{:S(2)}, u32[]{:S(2)}) collective-permute-start(f32[8,128,64]{2,1,0:T(8,128)} %multiply_add_fusion.2), channel_id=1, source_target_pairs={{0,8},{8,16},{16,24},{24,32},{32,40},{40,48},{48,56},{56,64},{64,7... | collective-permute-start | bytes 786440 | tf_op jit(solution)/shard_map/while/body/eval_jaxpr/ppermute | solution.py:12
  487.7 11.6 %collective-permute-start = (f32[8,128,64]{2,1,0:T(8,128)}, f32[8,128,64]{2,1,0:T(8,128)S(1)}, u32[]{:S(2)}, u32[]{:S(2)}) collective-permute-start(f32[8,128,64]{2,1,0:T(8,128)} %multiply_add_fusion.2), channel_id=1, source_target_pairs={{0,8},{8,16},{16,24},{24,32},{32,40},{40,48},{48,56},{56,64},{64,7... | collective-permute-start | bytes 786440 | tf_op jit(solution)/shard_map/while/body/eval_jaxpr/ppermute | solution.py:12
  500.3 12.4 %collective-permute-start = (f32[8,128,64]{2,1,0:T(8,128)}, f32[8,128,64]{2,1,0:T(8,128)S(1)}, u32[]{:S(2)}, u32[]{:S(2)}) collective-permute-start(f32[8,128,64]{2,1,0:T(8,128)} %multiply_add_fusion.2), channel_id=1, source_target_pairs={{0,8},{8,16},{16,24},{24,32},{32,40},{40,48},{48,56},{56,64},{64,7... | collective-permute-start | bytes 786440 | tf_op jit(solution)/shard_map/while/body/eval_jaxpr/ppermute | solution.py:12
  513.5 13.7 %collective-permute-start = (f32[8,128,64]{2,1,0:T(8,128)}, f32[8,128,64]{2,1,0:T(8,128)S(1)}, u32[]{:S(2)}, u32[]{:S(2)}) collective-permute-start(f32[8,128,64]{2,1,0:T(8,128)} %multiply_add_fusion.2), channel_id=1, source_target_pairs={{0,8},{8,16},{16,24},{24,32},{32,40},{40,48},{48,56},{56,64},{64,7... | collective-permute-start | bytes 786440 | tf_op jit(solution)/shard_map/while/body/eval_jaxpr/ppermute | solution.py:12
  528.1 13.5 %collective-permute-start = (f32[8,128,64]{2,1,0:T(8,128)}, f32[8,128,64]{2,1,0:T(8,128)S(1)}, u32[]{:S(2)}, u32[]{:S(2)}) collective-permute-start(f32[8,128,64]{2,1,0:T(8,128)} %multiply_add_fusion.2), channel_id=1, source_target_pairs={{0,8},{8,16},{16,24},{24,32},{32,40},{40,48},{48,56},{56,64},{64,7... | collective-permute-start | bytes 786440 | tf_op jit(solution)/shard_map/while/body/eval_jaxpr/ppermute | solution.py:12
  542.5 15.6 %collective-permute-start = (f32[8,128,64]{2,1,0:T(8,128)}, f32[8,128,64]{2,1,0:T(8,128)S(1)}, u32[]{:S(2)}, u32[]{:S(2)}) collective-permute-start(f32[8,128,64]{2,1,0:T(8,128)} %multiply_add_fusion.2), channel_id=1, source_target_pairs={{0,8},{8,16},{16,24},{24,32},{32,40},{40,48},{48,56},{56,64},{64,7... | collective-permute-start | bytes 786440 | tf_op jit(solution)/shard_map/while/body/eval_jaxpr/ppermute | solution.py:12
  559.1 17.7 %collective-permute-start = (f32[8,128,64]{2,1,0:T(8,128)}, f32[8,128,64]{2,1,0:T(8,128)S(1)}, u32[]{:S(2)}, u32[]{:S(2)}) collective-permute-start(f32[8,128,64]{2,1,0:T(8,128)} %multiply_add_fusion.2), channel_id=1, source_target_pairs={{0,8},{8,16},{16,24},{24,32},{32,40},{40,48},{48,56},{56,64},{64,7... | collective-permute-start | bytes 786440 | tf_op jit(solution)/shard_map/while/body/eval_jaxpr/ppermute | solution.py:12
  577.7 19.4 %collective-permute-start = (f32[8,128,64]{2,1,0:T(8,128)}, f32[8,128,64]{2,1,0:T(8,128)S(1)}, u32[]{:S(2)}, u32[]{:S(2)}) collective-permute-start(f32[8,128,64]{2,1,0:T(8,128)} %multiply_add_fusion.2), channel_id=1, source_target_pairs={{0,8},{8,16},{16,24},{24,32},{32,40},{40,48},{48,56},{56,64},{64,7... | collective-permute-start | bytes 786440 | tf_op jit(solution)/shard_map/while/body/eval_jaxpr/ppermute | solution.py:12
  598.0 18.8 %collective-permute-start = (f32[8,128,64]{2,1,0:T(8,128)}, f32[8,128,64]{2,1,0:T(8,128)S(1)}, u32[]{:S(2)}, u32[]{:S(2)}) collective-permute-start(f32[8,128,64]{2,1,0:T(8,128)} %multiply_add_fusion.2), channel_id=1, source_target_pairs={{0,8},{8,16},{16,24},{24,32},{32,40},{40,48},{48,56},{56,64},{64,7... | collective-permute-start | bytes 786440 | tf_op jit(solution)/shard_map/while/body/eval_jaxpr/ppermute | solution.py:12
  617.7 16.6 %collective-permute-start = (f32[8,128,64]{2,1,0:T(8,128)}, f32[8,128,64]{2,1,0:T(8,128)S(1)}, u32[]{:S(2)}, u32[]{:S(2)}) collective-permute-start(f32[8,128,64]{2,1,0:T(8,128)} %multiply_add_fusion.2), channel_id=1, source_target_pairs={{0,8},{8,16},{16,24},{24,32},{32,40},{40,48},{48,56},{56,64},{64,7... | collective-permute-start | bytes 786440 | tf_op jit(solution)/shard_map/while/body/eval_jaxpr/ppermute | solution.py:12
  635.3 14.9 %collective-permute-start = (f32[8,128,64]{2,1,0:T(8,128)}, f32[8,128,64]{2,1,0:T(8,128)S(1)}, u32[]{:S(2)}, u32[]{:S(2)}) collective-permute-start(f32[8,128,64]{2,1,0:T(8,128)} %multiply_add_fusion.2), channel_id=1, source_target_pairs={{0,8},{8,16},{16,24},{24,32},{32,40},{40,48},{48,56},{56,64},{64,7... | collective-permute-start | bytes 786440 | tf_op jit(solution)/shard_map/while/body/eval_jaxpr/ppermute | solution.py:12
  651.1 12.9 %collective-permute-start = (f32[8,128,64]{2,1,0:T(8,128)}, f32[8,128,64]{2,1,0:T(8,128)S(1)}, u32[]{:S(2)}, u32[]{:S(2)}) collective-permute-start(f32[8,128,64]{2,1,0:T(8,128)} %multiply_add_fusion.2), channel_id=1, source_target_pairs={{0,8},{8,16},{16,24},{24,32},{32,40},{40,48},{48,56},{56,64},{64,7... | collective-permute-start | bytes 786440 | tf_op jit(solution)/shard_map/while/body/eval_jaxpr/ppermute | solution.py:12
  676.6 11.6 %collective-permute-start = (f32[8,128,64]{2,1,0:T(8,128)}, f32[8,128,64]{2,1,0:T(8,128)S(1)}, u32[]{:S(2)}, u32[]{:S(2)}) collective-permute-start(f32[8,128,64]{2,1,0:T(8,128)} %multiply_add_fusion.2), channel_id=1, source_target_pairs={{0,8},{8,16},{16,24},{24,32},{32,40},{40,48},{48,56},{56,64},{64,7... | collective-permute-start | bytes 786440 | tf_op jit(solution)/shard_map/while/body/eval_jaxpr/ppermute | solution.py:12
  689.1 11.4 %collective-permute-start = (f32[8,128,64]{2,1,0:T(8,128)}, f32[8,128,64]{2,1,0:T(8,128)S(1)}, u32[]{:S(2)}, u32[]{:S(2)}) collective-permute-start(f32[8,128,64]{2,1,0:T(8,128)} %multiply_add_fusion.2), channel_id=1, source_target_pairs={{0,8},{8,16},{16,24},{24,32},{32,40},{40,48},{48,56},{56,64},{64,7... | collective-permute-start | bytes 786440 | tf_op jit(solution)/shard_map/while/body/eval_jaxpr/ppermute | solution.py:12
  (27 other events, 1237.1 us)
Sparse Core Ops, SparseCore 0:
  9.9 75.0 all-gather.9
  86.8 41.0 all-gather.5
  130.5 78.7 all-gather.7
  211.7 75.2 all-gather.11
  793.5 73.4 reduce-scatter.1
where the time goes:
time: 878 us; the launch traced here: 876 us
  waiting for transfers between devices  483 us (55%)
  starting transfers between devices  162 us (18%)
  blocking collectives  90.2 us (10%)
  other arithmetic  68 us (8%)
  local copies, waits for them, and re-layouts  29.4 us (3%)
  matrix products  28.5 us (3%)
  between operations  13.5 us (2%)
    ppermute x33, waiting for transfers between devices, passed_along(): return lax.ppermute(value, axis, pairs)  270 us
    ppermute x33, starting transfers between devices, passed_along(): return lax.ppermute(value, axis, pairs)  162 us
    reduce_scatter x1, waiting for transfers between devices, on_device(): lax.psum_scatter(partial_out, 'tp', scatter_dimension=1, tiled=True)  72.8 us
    all_gather x1, waiting for transfers between devices, on_device(): lax.all_gather(w_inner, 'seq', axis=0, tiled=True)  67.3 us
    psum x1, blocking collectives, on_device(): squares = lax.psum(jnp.sum(gated * gated, axis=1), 'tp')  48.3 us
    all_gather x1, waiting for transfers between devices, on_device(): whole = lax.all_gather(tokens, 'tp', axis=1, tiled=True)  42.9 us
    all_gather x1, blocking collectives, on_device(): lax.all_gather(w_step, 'seq', axis=0, tiled=True)  41.9 us
    add x31, other arithmetic, relay(): block_gain[:, None, None] * entering_now + block_state  28.2 us
  transfers between devices with their start and end apart: 38, of which 35 were waited for; matrix products, arithmetic and copies ran while one was open for 13% of the time, Pallas kernels for 0%

commit v1 on v0

--- a/solution.py
+++ b/solution.py
@@ -61,7 +61,9 @@
     local_valid = lax.dynamic_slice_in_dim(valid_rows, seq_index * local_blocks, local_blocks)
     in_block = jnp.arange(row_count, dtype=jnp.int32) % BLOCK
     carry_on = jnp.repeat(local_start == 0, BLOCK)
-    whole = lax.all_gather(tokens, "tp", axis=1, tiled=True)
+    length = lax.axis_size("tp")
+    repeats = [length if d == 1 else 1 for d in range(tokens.ndim)]
+    whole = lax.all_to_all(jnp.tile(tokens, repeats), "tp", split_axis=1, concat_axis=1, tiled=True)
     pieces = (
         lax.all_gather(w_inner, "seq", axis=0, tiled=True),
         lax.all_gather(w_states, "seq", axis=0, tiled=True),

time: 878 us -> 838 us (0.954)
  waiting for transfers between devices: 483 us -> 429 us
  starting transfers between devices: 162 us -> 172 us
    all_gather x1 -> x0, waiting for transfers between devices: 42.9 us -> none  [on_device(): whole = lax.all_gather(tokens, 'tp', axis=1, tiled=True)]
    all_gather x1, waiting for transfers between devices: 27.5 us -> 11.1 us  [on_device(): lax.all_gather(w_states, 'seq', axis=0, tiled=True)]
  transfers between devices with their start and end apart: 38 -> 38, of which waited for: 35 -> 35; matrix products, arithmetic and copies ran while one was open for 13% -> 14% of each run, Pallas kernels for 0% -> 0%
where the time goes in v1:
time: 838 us; the launch traced here: 835 us
  waiting for transfers between devices  429 us (51%)
  starting transfers between devices  172 us (21%)
  blocking collectives  89.6 us (11%)
  other arithmetic  66.6 us (8%)
  local copies, waits for them, and re-layouts  36.4 us (4%)
  matrix products  28 us (3%)
  between operations  13.6 us (2%)
    ppermute x33, waiting for transfers between devices, passed_along(): return lax.ppermute(value, axis, pairs)  269 us
    ppermute x33, starting transfers between devices, passed_along(): return lax.ppermute(value, axis, pairs)  164 us
    reduce_scatter x1, waiting for transfers between devices, on_device(): lax.psum_scatter(partial_out, 'tp', scatter_dimension=1, tiled=True)  72.1 us
    all_gather x1, waiting for transfers between devices, on_device(): lax.all_gather(w_inner, 'seq', axis=0, tiled=True)  70.5 us
    psum x1, blocking collectives, on_device(): squares = lax.psum(jnp.sum(gated * gated, axis=1), 'tp')  47.7 us
    all_gather x1, blocking collectives, on_device(): lax.all_gather(w_step, 'seq', axis=0, tiled=True)  41.9 us
    add x31, other arithmetic, relay(): block_gain[:, None, None] * entering_now + block_state  28.2 us
  transfers between devices with their start and end apart: 38, of which 35 were waited for; matrix products, arithmetic and copies ran while one was open for 14% of the time, Pallas kernels for 0%

profile of v1, /device:TPU:1, one launch (start us, length us, event | category | flops | bytes accessed | tf_op | source)
XLA Modules:
  0.0 835.3 jit_solution(4307910220471223635)
XLA Ops:
  11.3 7.8 all-to-all-start
  20.3 41.9 %all-gather = bf16[32,64,8]{1,2,0:T(8,128)(2,1)S(1)} all-gather(bf16[1,64,8]{1,2,0:T(8,128)(2,1)S(1)} %bitcast.103), channel_id=1, replica_groups=mesh['seq'=32,'tp'=8] {'seq'}, dimensions={0}, use_global_device_ids=true | all-gather | bytes 33792 | tf_op jit(solution)/shard_map/all_gather | solution.py:70
  74.4 11.1 %all-gather.7.cloned.1.call-done = bf16[2048,256]{1,0:T(8,128)(2,1)} async-done(((bf16[64,256]{1,0:T(8,128)(2,1)}), bf16[2048,256]{1,0:T(8,128)(2,1)}) %all-gather.7.cloned.1.call-update) | async-done | bytes 1048592 | tf_op jit(solution)/shard_map/all_gather | solution.py:69
  98.0 70.5 %all-gather.5.cloned.1.call-done = bf16[2048,2,512]{2,1,0:T(2,128)(2,1)} async-done(((bf16[64,2,512]{2,1,0:T(2,128)(2,1)}), bf16[2048,2,512]{2,1,0:T(2,128)(2,1)}) %all-gather.5.cloned.1.call-update) | async-done | bytes 4194320 | tf_op jit(solution)/shard_map/all_gather | solution.py:68
  204.6 456.6 %while.35 = (s32[]{:T(128)}, f32[8,128,64]{2,1,0:T(8,128)S(1)}, f32[8]{0:T(128)S(1)}, f32[8,128,64]{2,1,0:T(8,128)S(1)}, s32[]{:T(128)}) while((s32[]{:T(128)}, f32[8,128,64]{2,1,0:T(8,128)S(1)}, f32[8]{0:T(128)S(1)}, f32[8,128,64]{2,1,0:T(8,128)S(1)}, s32[]{:T(128)}) %tuple.79), condition=%wide.region_7.8_spmd, body=%wide.region_6.7_spmd.sunk | while | flops 131074 | bytes 1835141 | solution.py:125
  208.9 7.4 collective-permute-done
  221.3 10.2 %collective-permute-done = f32[8,128,64]{2,1,0:T(8,128)S(1)} collective-permute-done((f32[8,128,64]{2,1,0:T(8,128)}, f32[8,128,64]{2,1,0:T(8,128)S(1)}, u32[]{:S(2)}, u32[]{:S(2)}) %collective-permute-start) | collective-permute-done | bytes 262176 | tf_op jit(solution)/shard_map/while/body/eval_jaxpr/ppermute | solution.py:12
  237.2 11.4 %collective-permute-done = f32[8,128,64]{2,1,0:T(8,128)S(1)} collective-permute-done((f32[8,128,64]{2,1,0:T(8,128)}, f32[8,128,64]{2,1,0:T(8,128)S(1)}, u32[]{:S(2)}, u32[]{:S(2)}) %collective-permute-start) | collective-permute-done | bytes 262176 | tf_op jit(solution)/shard_map/while/body/eval_jaxpr/ppermute | solution.py:12
  276.0 7.3 collective-permute-done
  288.0 8.5 %collective-permute-done = f32[8,128,64]{2,1,0:T(8,128)S(1)} collective-permute-done((f32[8,128,64]{2,1,0:T(8,128)}, f32[8,128,64]{2,1,0:T(8,128)S(1)}, u32[]{:S(2)}, u32[]{:S(2)}) %collective-permute-start) | collective-permute-done | bytes 262176 | tf_op jit(solution)/shard_map/while/body/eval_jaxpr/ppermute | solution.py:12
  303.3 10.1 %collective-permute-done = f32[8,128,64]{2,1,0:T(8,128)S(1)} collective-permute-done((f32[8,128,64]{2,1,0:T(8,128)}, f32[8,128,64]{2,1,0:T(8,128)S(1)}, u32[]{:S(2)}, u32[]{:S(2)}) %collective-permute-start) | collective-permute-done | bytes 262176 | tf_op jit(solution)/shard_map/while/body/eval_jaxpr/ppermute | solution.py:12
  320.1 11.2 %collective-permute-done = f32[8,128,64]{2,1,0:T(8,128)S(1)} collective-permute-done((f32[8,128,64]{2,1,0:T(8,128)}, f32[8,128,64]{2,1,0:T(8,128)S(1)}, u32[]{:S(2)}, u32[]{:S(2)}) %collective-permute-start) | collective-permute-done | bytes 262176 | tf_op jit(solution)/shard_map/while/body/eval_jaxpr/ppermute | solution.py:12
  338.1 11.6 %collective-permute-done = f32[8,128,64]{2,1,0:T(8,128)S(1)} collective-permute-done((f32[8,128,64]{2,1,0:T(8,128)}, f32[8,128,64]{2,1,0:T(8,128)S(1)}, u32[]{:S(2)}, u32[]{:S(2)}) %collective-permute-start) | collective-permute-done | bytes 262176 | tf_op jit(solution)/shard_map/while/body/eval_jaxpr/ppermute | solution.py:12
  355.9 10.5 %collective-permute-done = f32[8,128,64]{2,1,0:T(8,128)S(1)} collective-permute-done((f32[8,128,64]{2,1,0:T(8,128)}, f32[8,128,64]{2,1,0:T(8,128)S(1)}, u32[]{:S(2)}, u32[]{:S(2)}) %collective-permute-start) | collective-permute-done | bytes 262176 | tf_op jit(solution)/shard_map/while/body/eval_jaxpr/ppermute | solution.py:12
  371.6 9.3 %collective-permute-done = f32[8,128,64]{2,1,0:T(8,128)S(1)} collective-permute-done((f32[8,128,64]{2,1,0:T(8,128)}, f32[8,128,64]{2,1,0:T(8,128)S(1)}, u32[]{:S(2)}, u32[]{:S(2)}) %collective-permute-start) | collective-permute-done | bytes 262176 | tf_op jit(solution)/shard_map/while/body/eval_jaxpr/ppermute | solution.py:12
  387.1 8.4 %collective-permute-done = f32[8,128,64]{2,1,0:T(8,128)S(1)} collective-permute-done((f32[8,128,64]{2,1,0:T(8,128)}, f32[8,128,64]{2,1,0:T(8,128)S(1)}, u32[]{:S(2)}, u32[]{:S(2)}) %collective-permute-start) | collective-permute-done | bytes 262176 | tf_op jit(solution)/shard_map/while/body/eval_jaxpr/ppermute | solution.py:12
  401.7 7.6 collective-permute-done
  479.7 8.4 %collective-permute-done = f32[8,128,64]{2,1,0:T(8,128)S(1)} collective-permute-done((f32[8,128,64]{2,1,0:T(8,128)}, f32[8,128,64]{2,1,0:T(8,128)S(1)}, u32[]{:S(2)}, u32[]{:S(2)}) %collective-permute-start) | collective-permute-done | bytes 262176 | tf_op jit(solution)/shard_map/while/body/eval_jaxpr/ppermute | solution.py:12
  494.8 9.5 %collective-permute-done = f32[8,128,64]{2,1,0:T(8,128)S(1)} collective-permute-done((f32[8,128,64]{2,1,0:T(8,128)}, f32[8,128,64]{2,1,0:T(8,128)S(1)}, u32[]{:S(2)}, u32[]{:S(2)}) %collective-permute-start) | collective-permute-done | bytes 262176 | tf_op jit(solution)/shard_map/while/body/eval_jaxpr/ppermute | solution.py:12
  509.9 10.1 %collective-permute-done = f32[8,128,64]{2,1,0:T(8,128)S(1)} collective-permute-done((f32[8,128,64]{2,1,0:T(8,128)}, f32[8,128,64]{2,1,0:T(8,128)S(1)}, u32[]{:S(2)}, u32[]{:S(2)}) %collective-permute-start) | collective-permute-done | bytes 262176 | tf_op jit(solution)/shard_map/while/body/eval_jaxpr/ppermute | solution.py:12
  526.0 10.8 %collective-permute-done = f32[8,128,64]{2,1,0:T(8,128)S(1)} collective-permute-done((f32[8,128,64]{2,1,0:T(8,128)}, f32[8,128,64]{2,1,0:T(8,128)S(1)}, u32[]{:S(2)}, u32[]{:S(2)}) %collective-permute-start) | collective-permute-done | bytes 262176 | tf_op jit(solution)/shard_map/while/body/eval_jaxpr/ppermute | solution.py:12
  542.1 11.3 %collective-permute-done = f32[8,128,64]{2,1,0:T(8,128)S(1)} collective-permute-done((f32[8,128,64]{2,1,0:T(8,128)}, f32[8,128,64]{2,1,0:T(8,128)S(1)}, u32[]{:S(2)}, u32[]{:S(2)}) %collective-permute-start) | collective-permute-done | bytes 262176 | tf_op jit(solution)/shard_map/while/body/eval_jaxpr/ppermute | solution.py:12
  554.4 7.3 collective-permute-start
  561.7 11.6 %collective-permute-done = f32[8,128,64]{2,1,0:T(8,128)S(1)} collective-permute-done((f32[8,128,64]{2,1,0:T(8,128)}, f32[8,128,64]{2,1,0:T(8,128)S(1)}, u32[]{:S(2)}, u32[]{:S(2)}) %collective-permute-start) | collective-permute-done | bytes 262176 | tf_op jit(solution)/shard_map/while/body/eval_jaxpr/ppermute | solution.py:12
  574.2 7.3 collective-permute-start
  581.6 10.5 %collective-permute-done = f32[8,128,64]{2,1,0:T(8,128)S(1)} collective-permute-done((f32[8,128,64]{2,1,0:T(8,128)}, f32[8,128,64]{2,1,0:T(8,128)S(1)}, u32[]{:S(2)}, u32[]{:S(2)}) %collective-permute-start) | collective-permute-done | bytes 262176 | tf_op jit(solution)/shard_map/while/body/eval_jaxpr/ppermute | solution.py:12
  599.5 9.3 %collective-permute-done = f32[8,128,64]{2,1,0:T(8,128)S(1)} collective-permute-done((f32[8,128,64]{2,1,0:T(8,128)}, f32[8,128,64]{2,1,0:T(8,128)S(1)}, u32[]{:S(2)}, u32[]{:S(2)}) %collective-permute-start) | collective-permute-done | bytes 262176 | tf_op jit(solution)/shard_map/while/body/eval_jaxpr/ppermute | solution.py:12
  615.3 8.2 collective-permute-done
  661.2 15.3 %while.36 = (s32[]{:T(128)}, f32[8,128,64]{2,1,0:T(8,128)S(1)}, bf16[4,8,128,64]{3,2,1,0:T(8,128)(2,1)}, f32[4,8]{1,0:T(4,128)S(1)}, f32[4]{0:T(128)S(1)}, /*index=5*/f32[4,8,128,64]{3,2,1,0:T(8,128)}, s32[]{:T(128)}) while((s32[]{:T(128)}, f32[8,128,64]{2,1,0:T(8,128)S(1)}, bf16[4,8,128,64]{3,2,1,0:T(8,128)(2,1)}, f32[4,8]{1,0:T(4,128)S(1)}, ...), condition=%wide.region_9.10_spmd, body=%wide.region_8.9_spmd.sunk | while | flops 262146 | bytes 1574085 | solution.py:132
  697.9 47.7 %psum.7 = f32[1024]{0:T(1024)S(1)} all-reduce(f32[1024]{0:T(1024)S(1)} %get-tuple-element.207), channel_id=1, replica_groups=mesh['seq'=32,'tp'=8] {'tp'}, use_global_device_ids=true, to_apply=%region_11.12 | all-reduce | flops 1024 | bytes 8192 | tf_op jit(solution)/shard_map/psum | solution.py:141
  745.7 7.9 fusion.26
  754.5 72.1 %reduce-scatter.2.cloned.1.call-done = f32[1024,256]{1,0:T(8,128)} async-done(((f32[1024,2048]{1,0:T(8,128)}), f32[1024,256]{1,0:T(8,128)}) %reduce-scatter.2.cloned.1.call-update) | async-done | bytes 1048592 | tf_op jit(solution)/shard_map/reduce_scatter | solution.py:149
  (225 shorter events, 351.5 us)
Async XLA Ops:
  6.5 78.9 %all-gather.7.cloned.1.call-start = ((), (), s32[]{:S(2)}) async-start(), calls=%async_computation.3 | async-start | bytes 1081344 | tf_op jit(solution)/shard_map/all_gather | solution.py:69
  7.3 161.2 %all-gather.5.cloned.1.call-start = ((), (), s32[]{:S(2)}) async-start(), calls=%async_computation.2 | async-start | bytes 4325376 | tf_op jit(solution)/shard_map/all_gather | solution.py:68
  11.3 56.6 %all-to-all-start = ((bf16[1024,8,256]{2,0,1:T(8,128)(2,1)}), bf16[1024,8,256]{2,0,1:T(8,128)(2,1)}, u32[]{:S(2)}, u32[]{:S(2)}) async-start(bf16[1024,8,256]{2,0,1:T(8,128)(2,1)} %tile.2), calls=%async_computation | async-start | bytes 8388608 | tf_op jit(solution)/shard_map/all_to_all | solution.py:66
  19.1 726.5 %all-gather.9.cloned.1.call-start = ((), (), s32[]{:S(2)}) async-start(), calls=%async_computation.4 | async-start | bytes 2162688 | tf_op jit(solution)/shard_map/all_gather | solution.py:146
  19.9 806.7 %reduce-scatter.2.cloned.1.call-start = ((), (), s32[]{:S(2)}) async-start(), calls=%async_computation.5 | async-start | bytes 9437184 | tf_op jit(solution)/shard_map/reduce_scatter | solution.py:149
  217.2 14.2 %collective-permute-start = (f32[8,128,64]{2,1,0:T(8,128)}, f32[8,128,64]{2,1,0:T(8,128)S(1)}, u32[]{:S(2)}, u32[]{:S(2)}) collective-permute-start(f32[8,128,64]{2,1,0:T(8,128)} %multiply_add_fusion.2), channel_id=1, source_target_pairs={{0,8},{8,16},{16,24},{24,32},{32,40},{40,48},{48,56},{56,64},{64,7... | collective-permute-start | bytes 786440 | tf_op jit(solution)/shard_map/while/body/eval_jaxpr/ppermute | solution.py:12
  232.3 16.3 %collective-permute-start = (f32[8,128,64]{2,1,0:T(8,128)}, f32[8,128,64]{2,1,0:T(8,128)S(1)}, u32[]{:S(2)}, u32[]{:S(2)}) collective-permute-start(f32[8,128,64]{2,1,0:T(8,128)} %multiply_add_fusion.2), channel_id=1, source_target_pairs={{0,8},{8,16},{16,24},{24,32},{32,40},{40,48},{48,56},{56,64},{64,7... | collective-permute-start | bytes 786440 | tf_op jit(solution)/shard_map/while/body/eval_jaxpr/ppermute | solution.py:12
  284.3 12.2 %collective-permute-start = (f32[8,128,64]{2,1,0:T(8,128)}, f32[8,128,64]{2,1,0:T(8,128)S(1)}, u32[]{:S(2)}, u32[]{:S(2)}) collective-permute-start(f32[8,128,64]{2,1,0:T(8,128)} %multiply_add_fusion.2), channel_id=1, source_target_pairs={{0,8},{8,16},{16,24},{24,32},{32,40},{40,48},{48,56},{56,64},{64,7... | collective-permute-start | bytes 786440 | tf_op jit(solution)/shard_map/while/body/eval_jaxpr/ppermute | solution.py:12
  297.4 16.0 %collective-permute-start = (f32[8,128,64]{2,1,0:T(8,128)}, f32[8,128,64]{2,1,0:T(8,128)S(1)}, u32[]{:S(2)}, u32[]{:S(2)}) collective-permute-start(f32[8,128,64]{2,1,0:T(8,128)} %multiply_add_fusion.2), channel_id=1, source_target_pairs={{0,8},{8,16},{16,24},{24,32},{32,40},{40,48},{48,56},{56,64},{64,7... | collective-permute-start | bytes 786440 | tf_op jit(solution)/shard_map/while/body/eval_jaxpr/ppermute | solution.py:12
  314.3 17.1 %collective-permute-start = (f32[8,128,64]{2,1,0:T(8,128)}, f32[8,128,64]{2,1,0:T(8,128)S(1)}, u32[]{:S(2)}, u32[]{:S(2)}) collective-permute-start(f32[8,128,64]{2,1,0:T(8,128)} %multiply_add_fusion.2), channel_id=1, source_target_pairs={{0,8},{8,16},{16,24},{24,32},{32,40},{40,48},{48,56},{56,64},{64,7... | collective-permute-start | bytes 786440 | tf_op jit(solution)/shard_map/while/body/eval_jaxpr/ppermute | solution.py:12
  332.3 17.5 %collective-permute-start = (f32[8,128,64]{2,1,0:T(8,128)}, f32[8,128,64]{2,1,0:T(8,128)S(1)}, u32[]{:S(2)}, u32[]{:S(2)}) collective-permute-start(f32[8,128,64]{2,1,0:T(8,128)} %multiply_add_fusion.2), channel_id=1, source_target_pairs={{0,8},{8,16},{16,24},{24,32},{32,40},{40,48},{48,56},{56,64},{64,7... | collective-permute-start | bytes 786440 | tf_op jit(solution)/shard_map/while/body/eval_jaxpr/ppermute | solution.py:12
  350.6 15.7 %collective-permute-start = (f32[8,128,64]{2,1,0:T(8,128)}, f32[8,128,64]{2,1,0:T(8,128)S(1)}, u32[]{:S(2)}, u32[]{:S(2)}) collective-permute-start(f32[8,128,64]{2,1,0:T(8,128)} %multiply_add_fusion.2), channel_id=1, source_target_pairs={{0,8},{8,16},{16,24},{24,32},{32,40},{40,48},{48,56},{56,64},{64,7... | collective-permute-start | bytes 786440 | tf_op jit(solution)/shard_map/while/body/eval_jaxpr/ppermute | solution.py:12
  367.2 13.7 %collective-permute-start = (f32[8,128,64]{2,1,0:T(8,128)}, f32[8,128,64]{2,1,0:T(8,128)S(1)}, u32[]{:S(2)}, u32[]{:S(2)}) collective-permute-start(f32[8,128,64]{2,1,0:T(8,128)} %multiply_add_fusion.2), channel_id=1, source_target_pairs={{0,8},{8,16},{16,24},{24,32},{32,40},{40,48},{48,56},{56,64},{64,7... | collective-permute-start | bytes 786440 | tf_op jit(solution)/shard_map/while/body/eval_jaxpr/ppermute | solution.py:12
  381.8 13.7 %collective-permute-start = (f32[8,128,64]{2,1,0:T(8,128)}, f32[8,128,64]{2,1,0:T(8,128)S(1)}, u32[]{:S(2)}, u32[]{:S(2)}) collective-permute-start(f32[8,128,64]{2,1,0:T(8,128)} %multiply_add_fusion.2), channel_id=1, source_target_pairs={{0,8},{8,16},{16,24},{24,32},{32,40},{40,48},{48,56},{56,64},{64,7... | collective-permute-start | bytes 786440 | tf_op jit(solution)/shard_map/while/body/eval_jaxpr/ppermute | solution.py:12
  396.4 12.8 %collective-permute-start = (f32[8,128,64]{2,1,0:T(8,128)}, f32[8,128,64]{2,1,0:T(8,128)S(1)}, u32[]{:S(2)}, u32[]{:S(2)}) collective-permute-start(f32[8,128,64]{2,1,0:T(8,128)} %multiply_add_fusion.2), channel_id=1, source_target_pairs={{0,8},{8,16},{16,24},{24,32},{32,40},{40,48},{48,56},{56,64},{64,7... | collective-permute-start | bytes 786440 | tf_op jit(solution)/shard_map/while/body/eval_jaxpr/ppermute | solution.py:12
  410.2 12.0 %collective-permute-start = (f32[8,128,64]{2,1,0:T(8,128)}, f32[8,128,64]{2,1,0:T(8,128)S(1)}, u32[]{:S(2)}, u32[]{:S(2)}) collective-permute-start(f32[8,128,64]{2,1,0:T(8,128)} %multiply_add_fusion.2), channel_id=1, source_target_pairs={{0,8},{8,16},{16,24},{24,32},{32,40},{40,48},{48,56},{56,64},{64,7... | collective-permute-start | bytes 786440 | tf_op jit(solution)/shard_map/while/body/eval_jaxpr/ppermute | solution.py:12
  423.1 11.6 %collective-permute-start = (f32[8,128,64]{2,1,0:T(8,128)}, f32[8,128,64]{2,1,0:T(8,128)S(1)}, u32[]{:S(2)}, u32[]{:S(2)}) collective-permute-start(f32[8,128,64]{2,1,0:T(8,128)} %multiply_add_fusion.2), channel_id=1, source_target_pairs={{0,8},{8,16},{16,24},{24,32},{32,40},{40,48},{48,56},{56,64},{64,7... | collective-permute-start | bytes 786440 | tf_op jit(solution)/shard_map/while/body/eval_jaxpr/ppermute | solution.py:12
  435.6 11.6 %collective-permute-start = (f32[8,128,64]{2,1,0:T(8,128)}, f32[8,128,64]{2,1,0:T(8,128)S(1)}, u32[]{:S(2)}, u32[]{:S(2)}) collective-permute-start(f32[8,128,64]{2,1,0:T(8,128)} %multiply_add_fusion.2), channel_id=1, source_target_pairs={{0,8},{8,16},{16,24},{24,32},{32,40},{40,48},{48,56},{56,64},{64,7... | collective-permute-start | bytes 786440 | tf_op jit(solution)/shard_map/while/body/eval_jaxpr/ppermute | solution.py:12
  448.1 11.7 %collective-permute-start = (f32[8,128,64]{2,1,0:T(8,128)}, f32[8,128,64]{2,1,0:T(8,128)S(1)}, u32[]{:S(2)}, u32[]{:S(2)}) collective-permute-start(f32[8,128,64]{2,1,0:T(8,128)} %multiply_add_fusion.2), channel_id=1, source_target_pairs={{0,8},{8,16},{16,24},{24,32},{32,40},{40,48},{48,56},{56,64},{64,7... | collective-permute-start | bytes 786440 | tf_op jit(solution)/shard_map/while/body/eval_jaxpr/ppermute | solution.py:12
  460.7 12.5 %collective-permute-start = (f32[8,128,64]{2,1,0:T(8,128)}, f32[8,128,64]{2,1,0:T(8,128)S(1)}, u32[]{:S(2)}, u32[]{:S(2)}) collective-permute-start(f32[8,128,64]{2,1,0:T(8,128)} %multiply_add_fusion.2), channel_id=1, source_target_pairs={{0,8},{8,16},{16,24},{24,32},{32,40},{40,48},{48,56},{56,64},{64,7... | collective-permute-start | bytes 786440 | tf_op jit(solution)/shard_map/while/body/eval_jaxpr/ppermute | solution.py:12
  474.2 14.0 %collective-permute-start = (f32[8,128,64]{2,1,0:T(8,128)}, f32[8,128,64]{2,1,0:T(8,128)S(1)}, u32[]{:S(2)}, u32[]{:S(2)}) collective-permute-start(f32[8,128,64]{2,1,0:T(8,128)} %multiply_add_fusion.2), channel_id=1, source_target_pairs={{0,8},{8,16},{16,24},{24,32},{32,40},{40,48},{48,56},{56,64},{64,7... | collective-permute-start | bytes 786440 | tf_op jit(solution)/shard_map/while/body/eval_jaxpr/ppermute | solution.py:12
  489.1 15.3 %collective-permute-start = (f32[8,128,64]{2,1,0:T(8,128)}, f32[8,128,64]{2,1,0:T(8,128)S(1)}, u32[]{:S(2)}, u32[]{:S(2)}) collective-permute-start(f32[8,128,64]{2,1,0:T(8,128)} %multiply_add_fusion.2), channel_id=1, source_target_pairs={{0,8},{8,16},{16,24},{24,32},{32,40},{40,48},{48,56},{56,64},{64,7... | collective-permute-start | bytes 786440 | tf_op jit(solution)/shard_map/while/body/eval_jaxpr/ppermute | solution.py:12
  505.3 14.7 %collective-permute-start = (f32[8,128,64]{2,1,0:T(8,128)}, f32[8,128,64]{2,1,0:T(8,128)S(1)}, u32[]{:S(2)}, u32[]{:S(2)}) collective-permute-start(f32[8,128,64]{2,1,0:T(8,128)} %multiply_add_fusion.2), channel_id=1, source_target_pairs={{0,8},{8,16},{16,24},{24,32},{32,40},{40,48},{48,56},{56,64},{64,7... | collective-permute-start | bytes 786440 | tf_op jit(solution)/shard_map/while/body/eval_jaxpr/ppermute | solution.py:12
  520.9 15.9 %collective-permute-start = (f32[8,128,64]{2,1,0:T(8,128)}, f32[8,128,64]{2,1,0:T(8,128)S(1)}, u32[]{:S(2)}, u32[]{:S(2)}) collective-permute-start(f32[8,128,64]{2,1,0:T(8,128)} %multiply_add_fusion.2), channel_id=1, source_target_pairs={{0,8},{8,16},{16,24},{24,32},{32,40},{40,48},{48,56},{56,64},{64,7... | collective-permute-start | bytes 786440 | tf_op jit(solution)/shard_map/while/body/eval_jaxpr/ppermute | solution.py:12
  537.7 15.7 %collective-permute-start = (f32[8,128,64]{2,1,0:T(8,128)}, f32[8,128,64]{2,1,0:T(8,128)S(1)}, u32[]{:S(2)}, u32[]{:S(2)}) collective-permute-start(f32[8,128,64]{2,1,0:T(8,128)} %multiply_add_fusion.2), channel_id=1, source_target_pairs={{0,8},{8,16},{16,24},{24,32},{32,40},{40,48},{48,56},{56,64},{64,7... | collective-permute-start | bytes 786440 | tf_op jit(solution)/shard_map/while/body/eval_jaxpr/ppermute | solution.py:12
  554.4 19.0 %collective-permute-start = (f32[8,128,64]{2,1,0:T(8,128)}, f32[8,128,64]{2,1,0:T(8,128)S(1)}, u32[]{:S(2)}, u32[]{:S(2)}) collective-permute-start(f32[8,128,64]{2,1,0:T(8,128)} %multiply_add_fusion.2), channel_id=1, source_target_pairs={{0,8},{8,16},{16,24},{24,32},{32,40},{40,48},{48,56},{56,64},{64,7... | collective-permute-start | bytes 786440 | tf_op jit(solution)/shard_map/while/body/eval_jaxpr/ppermute | solution.py:12
  574.2 17.8 %collective-permute-start = (f32[8,128,64]{2,1,0:T(8,128)}, f32[8,128,64]{2,1,0:T(8,128)S(1)}, u32[]{:S(2)}, u32[]{:S(2)}) collective-permute-start(f32[8,128,64]{2,1,0:T(8,128)} %multiply_add_fusion.2), channel_id=1, source_target_pairs={{0,8},{8,16},{16,24},{24,32},{32,40},{40,48},{48,56},{56,64},{64,7... | collective-permute-start | bytes 786440 | tf_op jit(solution)/shard_map/while/body/eval_jaxpr/ppermute | solution.py:12
  593.0 15.9 %collective-permute-start = (f32[8,128,64]{2,1,0:T(8,128)}, f32[8,128,64]{2,1,0:T(8,128)S(1)}, u32[]{:S(2)}, u32[]{:S(2)}) collective-permute-start(f32[8,128,64]{2,1,0:T(8,128)} %multiply_add_fusion.2), channel_id=1, source_target_pairs={{0,8},{8,16},{16,24},{24,32},{32,40},{40,48},{48,56},{56,64},{64,7... | collective-permute-start | bytes 786440 | tf_op jit(solution)/shard_map/while/body/eval_jaxpr/ppermute | solution.py:12
  609.8 13.7 %collective-permute-start = (f32[8,128,64]{2,1,0:T(8,128)}, f32[8,128,64]{2,1,0:T(8,128)S(1)}, u32[]{:S(2)}, u32[]{:S(2)}) collective-permute-start(f32[8,128,64]{2,1,0:T(8,128)} %multiply_add_fusion.2), channel_id=1, source_target_pairs={{0,8},{8,16},{16,24},{24,32},{32,40},{40,48},{48,56},{56,64},{64,7... | collective-permute-start | bytes 786440 | tf_op jit(solution)/shard_map/while/body/eval_jaxpr/ppermute | solution.py:12
  624.4 12.0 %collective-permute-start = (f32[8,128,64]{2,1,0:T(8,128)}, f32[8,128,64]{2,1,0:T(8,128)S(1)}, u32[]{:S(2)}, u32[]{:S(2)}) collective-permute-start(f32[8,128,64]{2,1,0:T(8,128)} %multiply_add_fusion.2), channel_id=1, source_target_pairs={{0,8},{8,16},{16,24},{24,32},{32,40},{40,48},{48,56},{56,64},{64,7... | collective-permute-start | bytes 786440 | tf_op jit(solution)/shard_map/while/body/eval_jaxpr/ppermute | solution.py:12
  637.3 11.5 %collective-permute-start = (f32[8,128,64]{2,1,0:T(8,128)}, f32[8,128,64]{2,1,0:T(8,128)S(1)}, u32[]{:S(2)}, u32[]{:S(2)}) collective-permute-start(f32[8,128,64]{2,1,0:T(8,128)} %multiply_add_fusion.2), channel_id=1, source_target_pairs={{0,8},{8,16},{16,24},{24,32},{32,40},{40,48},{48,56},{56,64},{64,7... | collective-permute-start | bytes 786440 | tf_op jit(solution)/shard_map/while/body/eval_jaxpr/ppermute | solution.py:12
  649.8 11.4 %collective-permute-start = (f32[8,128,64]{2,1,0:T(8,128)}, f32[8,128,64]{2,1,0:T(8,128)S(1)}, u32[]{:S(2)}, u32[]{:S(2)}) collective-permute-start(f32[8,128,64]{2,1,0:T(8,128)} %multiply_add_fusion.2), channel_id=1, source_target_pairs={{0,8},{8,16},{16,24},{24,32},{32,40},{40,48},{48,56},{56,64},{64,7... | collective-permute-start | bytes 786440 | tf_op jit(solution)/shard_map/while/body/eval_jaxpr/ppermute | solution.py:12
  (33 other events, 1160.9 us)
Sparse Core Ops, SparseCore 0:
  9.9 75.4 all-gather.6
  88.1 80.3 all-gather.4
  171.0 75.2 all-gather.8
  753.7 72.7 reduce-scatter.1
